TPU v7x, 256 devices: a whole 4x4x8 slice. The times are simulated.
256 devices in a mesh: ctx: 32 (over z, x), tp: 8 (over y, core).
Axes of the slice: x: 4, y: 4, z: 8, core: 2. Of those that a mesh axis runs over, the one named last changes fastest.
Arguments:
- activations: bfloat16 [8192, 4096], P('ctx'), may hold values from -38 to 38
- w_qkv: bfloat16 [4096, 6144], P(None, 'tp'), may hold values from -0.09375 to 0.09375
- matching: int32 [8, 32], P('tp'), may hold values from 0 to 31, each once within a row
- dropout_bits: int32 [8192, 512], P('ctx', 'tp'), may hold values from 0 to 65535
- out_grad: bfloat16 [8192, 2048], P('ctx', 'tp'), may hold values from -0.29882812 to 0.29882812
Outputs:
- attended: bfloat16 [8192, 2048], P('ctx', 'tp')
- input_grad: bfloat16 [8192, 4096], P('ctx', 'tp')
- weight_grad: bfloat16 [4096, 6144], P('ctx', 'tp')
Inputs may be any that keep to these rules, and one draw needn't show every extreme that they name: Each row of matching is a permutation of the 32 blocks.
All inputs are finite; a program needn't handle non-finite values.
Results may differ from a plain program's by a relative error of at most 0.019.
Values may be sent and summed in bfloat16 or wider, within the bound.
No kernel may reach another device: no remote copies, remote signals or barrier semaphores. Data moves between devices by JAX's collectives and lax.ppermute only.
A program may use at most 128 MiB of HBM per device.

v0:
```python
import jax
import jax.numpy as jnp
import numpy as np
from jax import lax
from jax.sharding import PartitionSpec as P

HD = 128
BLK = 256
HGROUP = 2
WORDS = 32


def unpack_bits(words):
    shifts = jnp.arange(16, dtype=jnp.int32)
    bits = jnp.bitwise_and(jnp.right_shift(words[..., None], shifts), 1)
    return bits.reshape(words.shape[:-1] + (words.shape[-1] * 16,)).astype(jnp.float32) * 2.0


def to_blocks(flat, width):
    row_total = flat.shape[0]
    head_count = flat.shape[1] // width
    return flat.reshape(row_total // BLK, BLK, head_count, width).transpose(2, 0, 1, 3)


def from_blocks(blocked):
    head_count, block_count, block_rows, width = blocked.shape
    return blocked.transpose(1, 2, 0, 3).reshape(block_count * block_rows, head_count * width)


def pick_rows(current, shard_rows, wanted_rows, first_row):
    row_count = shard_rows.shape[0]
    head_count = wanted_rows.shape[0]
    width = shard_rows.shape[1] // head_count
    by_head = shard_rows.reshape(row_count, head_count, width).transpose(1, 0, 2)
    offset = wanted_rows.reshape(head_count, -1) - first_row
    within = (offset >= 0) & (offset < row_count)
    picked = jnp.take_along_axis(by_head, jnp.clip(offset, 0, row_count - 1)[:, :, None], axis=1)
    merged = jnp.where(within[:, :, None], picked, current.reshape(head_count, -1, width))
    return merged.reshape(current.shape)


def per_device(activations, w_qkv, matching, dropout_bits, out_grad):
    f32 = jnp.float32
    local_tokens = activations.shape[0]
    head_count = out_grad.shape[1] // HD
    local_blocks = local_tokens // BLK
    score_scale = HD ** (-0.5)
    ctx_index = lax.axis_index("ctx")
    projected = jnp.dot(activations, w_qkv, preferred_element_type=f32).astype(jnp.bfloat16)
    projected = projected.reshape(local_tokens, head_count, 3, HD)
    query_flat = projected[:, :, 0].reshape(local_tokens, head_count * HD)
    key_flat = projected[:, :, 1].reshape(local_tokens, head_count * HD)
    value_flat = projected[:, :, 2].reshape(local_tokens, head_count * HD)
    query = to_blocks(query_flat, HD)
    key_own = to_blocks(key_flat, HD)
    value_own = to_blocks(value_flat, HD)
    head_match = matching[np.arange(head_count) // HGROUP]
    all_blocks = head_match.shape[1]
    matched = lax.dynamic_slice_in_dim(head_match, ctx_index * local_blocks, local_blocks, 1)
    in_block = jnp.arange(BLK, dtype=jnp.int32)
    key_rows = matched[:, :, None] * BLK + in_block
    empty_rows = jnp.zeros((head_count, local_blocks, BLK, HD), jnp.bfloat16)
    first_row = jnp.int32(0)
    key_far = pick_rows(
        empty_rows, lax.all_gather(key_flat, "ctx", axis=0, tiled=True), key_rows, first_row
    )
    value_far = pick_rows(
        empty_rows, lax.all_gather(value_flat, "ctx", axis=0, tiled=True), key_rows, first_row
    )
    keys = jnp.concatenate([key_own, key_far], 2)
    values = jnp.concatenate([value_own, value_far], 2)
    scores = jnp.einsum("hnqd,hnkd->hnqk", query, keys, preferred_element_type=f32) * score_scale
    row_max = jnp.max(scores, -1, keepdims=True)
    log_total = row_max + jnp.log(jnp.sum(jnp.exp(scores - row_max), -1, keepdims=True))
    probability = jnp.exp(scores - log_total)
    kept = unpack_bits(to_blocks(dropout_bits, WORDS))
    dropped = (probability * kept).astype(jnp.bfloat16)
    attended = jnp.einsum("hnqk,hnkd->hnqd", dropped, values, preferred_element_type=f32).astype(
        jnp.bfloat16
    )
    grad_out = to_blocks(out_grad, HD)
    grad_prob = jnp.einsum("hnqd,hnkd->hnqk", grad_out, values, preferred_element_type=f32) * kept
    row_delta = jnp.sum(probability * grad_prob, -1, keepdims=True)
    grad_score = (probability * (grad_prob - row_delta) * score_scale).astype(jnp.bfloat16)
    grad_query = jnp.einsum("hnqk,hnkd->hnqd", grad_score, keys, preferred_element_type=f32).astype(
        jnp.bfloat16
    )
    grad_keys = jnp.einsum("hnqk,hnqd->hnkd", grad_score, query, preferred_element_type=f32)
    grad_values = jnp.einsum("hnqk,hnqd->hnkd", dropped, grad_out, preferred_element_type=f32)
    inverse = (
        jnp.zeros_like(head_match)
        .at[np.arange(head_count)[:, None], head_match]
        .set(jnp.broadcast_to(jnp.arange(all_blocks, dtype=jnp.int32)[None, :], head_match.shape))
    )
    sources = lax.dynamic_slice_in_dim(inverse, ctx_index * local_blocks, local_blocks, 1)
    query_rows = sources[:, :, None] * BLK + in_block
    far_part = jnp.concatenate([grad_keys[:, :, BLK:], grad_values[:, :, BLK:]], -1).astype(
        jnp.bfloat16
    )
    far_flat = from_blocks(far_part)
    empty_terms = jnp.zeros((head_count, local_blocks, BLK, 2 * HD), jnp.bfloat16)
    returned = pick_rows(
        empty_terms, lax.all_gather(far_flat, "ctx", axis=0, tiled=True), query_rows, jnp.int32(0)
    )
    far_key = returned[..., :HD].astype(f32)
    far_value = returned[..., HD:].astype(f32)
    grad_key = (grad_keys[:, :, :BLK] + far_key).astype(jnp.bfloat16)
    grad_value = (grad_values[:, :, :BLK] + far_value).astype(jnp.bfloat16)
    stacked = jnp.stack([grad_query, grad_key, grad_value], 3)
    grad_qkv = stacked.transpose(1, 2, 0, 3, 4).reshape(local_tokens, head_count * 3 * HD)
    weight_grad = lax.psum_scatter(
        lax.dot_general(
            activations, grad_qkv, (((0,), (0,)), ((), ())), preferred_element_type=f32
        ).astype(jnp.bfloat16),
        "ctx",
        scatter_dimension=0,
        tiled=True,
    )
    input_grad = lax.psum_scatter(
        lax.dot_general(w_qkv, grad_qkv, (((1,), (1,)), ((), ())), preferred_element_type=f32),
        "tp",
        scatter_dimension=0,
        tiled=True,
    ).T.astype(jnp.bfloat16)
    return (from_blocks(attended), input_grad, weight_grad)


def solution(mesh):
    return jax.shard_map(
        per_device,
        mesh=mesh,
        in_specs=(P("ctx", None), P(None, "tp"), P("tp", None), P("ctx", "tp"), P("ctx", "tp")),
        out_specs=(P("ctx", "tp"), P("ctx", "tp"), P("ctx", "tp")),
        check_vma=False,
    )
```

profile of v0, /device:TPU:8, one launch (start us, length us, event | category | flops | bytes accessed | tf_op | source)
XLA Modules:
  0.0 628.6 jit_solution(16482032936210440719)
XLA Ops:
  7.2 0.0 all-gather.4.cloned.1.call-start
  7.3 1.5 copy-done
  8.8 4.6 convolution_convert_fusion.1
  13.3 0.2 copy.44
  13.5 0.7 fusion.41
  14.2 0.0 all-gather.4.cloned.1.call-update
  14.3 0.0 all-gather.6.cloned.1.call-start
  14.3 0.7 all-gather.6.cloned.1.call-update
  15.0 0.0 all-gather.8.cloned.1.call-start
  15.1 1.0 copy.74
  16.1 1.7 copy.73
  17.8 0.6 fusion.42
  18.4 0.6 or_bitcast_fusion
  19.1 0.1 shift_right_arithmetic.28
  19.1 0.1 copy.69
  19.2 0.8 copy.72
  20.0 0.1 shift_right_arithmetic.25
  20.1 1.4 copy.49
  21.5 0.6 and_bitcast_fusion
  22.1 0.6 compare_and_fusion.2
  22.7 77.1 %all-gather.4.cloned.1.call-done = bf16[8192,256]{0,1:T(8,128)(2,1)} async-done(((bf16[256,256]{0,1:T(8,128)(2,1)}), bf16[8192,256]{0,1:T(8,128)(2,1)}) %all-gather.4.cloned.1.call-update) | async-done | bytes 4194320 | tf_op jit(solution)/shard_map/all_gather | solution.py:65
  99.9 6.3 %copy.48 = bf16[8192,2,128]{2,0,1:T(8,128)(2,1)} copy(bf16[8192,2,128]{0,2,1:T(8,128)(2,1)} %bitcast.125) | data formatting | bytes 8388608 | tf_op jit(solution)/shard_map/reshape | solution.py:34
  106.2 80.0 %all-gather.6.cloned.1.call-done = bf16[8192,256]{0,1:T(8,128)(2,1)} async-done(((bf16[256,256]{0,1:T(8,128)(2,1)}), bf16[8192,256]{0,1:T(8,128)(2,1)}) %all-gather.6.cloned.1.call-update) | async-done | bytes 4194320 | tf_op jit(solution)/shard_map/all_gather | solution.py:68
  186.2 6.4 %copy.52 = bf16[8192,2,128]{2,0,1:T(8,128)(2,1)} copy(bf16[8192,2,128]{0,2,1:T(8,128)(2,1)} %bitcast.126) | data formatting | bytes 8388608 | tf_op jit(solution)/shard_map/reshape | solution.py:34
  192.6 6.7 %gather_fusion.1 = bf16[512,128]{1,0:T(8,128)(2,1)S(1)} fusion(bf16[2,8192,128]{2,1,0:T(8,128)(2,1)} %bitcast.123, s32[512]{0:T(512)S(1)} %bitcast.118), kind=kCustom, calls=%fused_computation.clone | custom fusion | bytes 266240 | tf_op jit(solution)/shard_map/jit(take_along_axis)/gather | solution.py:37
  199.3 6.7 %gather_fusion.2 = bf16[512,128]{1,0:T(8,128)(2,1)S(1)} fusion(bf16[2,8192,128]{2,1,0:T(8,128)(2,1)} %bitcast.124, s32[512]{0:T(512)S(1)} %bitcast.119), kind=kCustom, calls=%fused_computation.1.clone | custom fusion | bytes 266240 | tf_op jit(solution)/shard_map/jit(take_along_axis)/gather | solution.py:37
  206.0 0.2 fusion.25
  206.2 0.6 copy-done.4
  206.9 1.3 fusion.43
  208.2 0.3 exponential_reduce_fusion
  208.6 1.5 multiply_convert_fusion
  210.1 0.8 copy-done.1
  210.9 1.0 convolution_bitcast_fusion.2
  211.9 2.6 fusion.5
  214.5 5.2 convolution_bitcast_fusion.3
  219.7 1.0 slice.70
  220.7 1.0 slice.69
  221.7 0.7 pad_maximum_fusion
  222.4 0.0 all-gather.8.cloned.1.call-update
  222.4 0.2 reduce-scatter.5.cloned.1.call-start
  222.7 0.1 reshape.379
  222.8 0.1 reshape.381
  222.9 3.5 scatter_fusion
  226.3 0.2 multiply_reduce_fusion.1
  226.5 0.1 fusion.30
  226.6 0.1 compare_and_fusion.1
  226.7 4.6 fusion.7
  231.3 94.2 %all-gather.8.cloned.1.call-done = bf16[8192,512]{0,1:T(8,128)(2,1)} async-done(((bf16[256,512]{0,1:T(8,128)(2,1)}), bf16[8192,512]{0,1:T(8,128)(2,1)}) %all-gather.8.cloned.1.call-update) | async-done | bytes 8388624 | tf_op jit(solution)/shard_map/all_gather | solution.py:103
  325.5 12.0 %copy.59 = bf16[8192,2,256]{2,0,1:T(8,128)(2,1)} copy(bf16[8192,2,256]{0,2,1:T(8,128)(2,1)} %bitcast.122) | data formatting | bytes 16777216 | tf_op jit(solution)/shard_map/reshape | solution.py:34
  337.5 6.9 %gather_fusion = bf16[512,256]{1,0:T(8,128)(2,1)S(1)} fusion(bf16[2,8192,256]{2,1,0:T(8,128)(2,1)} %bitcast.121, s32[512]{0:T(512)S(1)} %bitcast.120), kind=kCustom, calls=%fused_computation.2 | custom fusion | bytes 528384 | tf_op jit(solution)/shard_map/jit(take_along_axis)/gather | solution.py:37
  344.4 0.1 copy.60
  344.6 1.0 fusion.21
  345.7 6.6 %convolution_bitcast_fusion = f32[4096,256]{0,1:T(8,128)} fusion(bf16[256,768]{0,1:T(8,128)(2,1)S(1)} %bitcast.128, bf16[4096,768]{1,0:T(8,128)(2,1)} %param.12), kind=kOutput, calls=%fused_computation.7 | convolution fusion | flops 1610612736 | bytes 10878976 | tf_op jit(solution)/shard_map/dot_general | solution.py:120
  352.3 0.0 reduce-scatter.5.cloned.1.call-update
  352.3 0.0 reduce-scatter.7.cloned.1.call-start
  352.3 4.5 fusion.1
  356.8 8.6 %copy.70 = bf16[4096,768]{1,0:T(8,128)(2,1)} copy(bf16[4096,768]{0,1:T(8,128)(2,1)} %fusion.1) | data formatting | bytes 12582912
  365.4 0.0 reduce-scatter.7.cloned.1.call-update
  365.5 1.0 copy-done.2
  366.5 0.3 convolution_convert_fusion.3
  366.8 0.8 copy.62
  367.6 20.7 %reduce-scatter.5.cloned.1.call-done = f32[512,256]{0,1:T(8,128)} async-done(((f32[4096,256]{0,1:T(8,128)}), f32[512,256]{0,1:T(8,128)}) %reduce-scatter.5.cloned.1.call-update) | async-done | bytes 524304 | tf_op jit(solution)/shard_map/reduce_scatter | solution.py:119
  388.3 1.8 convert_bitcast_fusion
  390.0 232.0 %reduce-scatter.7.cloned.1.call-done = bf16[128,768]{1,0:T(8,128)(2,1)} async-done(((bf16[4096,768]{1,0:T(8,128)(2,1)}), bf16[128,768]{1,0:T(8,128)(2,1)}) %reduce-scatter.7.cloned.1.call-update) | async-done | bytes 196624
  (24 shorter events, 0.2 us)
Async XLA Ops:
  7.2 1.6 copy-start
  7.2 10.6 %copy-start.7 = (s32[1,32]{1,0:T(1,128)S(1)}, s32[1,32]{1,0:T(1,128)}, u32[]{:S(2)}) copy-start(s32[1,32]{1,0:T(1,128)} %param.13) | copy-start | bytes 388
  7.2 11.9 %copy-start.5 = (bf16[256,256]{1,0:T(8,128)(2,1)S(1)}, bf16[256,256]{1,0:T(8,128)(2,1)}, u32[]{:S(2)}) copy-start(bf16[256,256]{1,0:T(8,128)(2,1)} %param.15) | copy-start | bytes 393220
  7.2 12.8 %copy-start.6 = (s32[256,64]{0,1:T(8,128)S(1)}, s32[256,64]{0,1:T(8,128)}, u32[]{:S(2)}) copy-start(s32[256,64]{0,1:T(8,128)} %param.14) | copy-start | bytes 196612
  7.2 92.7 %all-gather.4.cloned.1.call-start = ((), (), s32[]{:S(2)}) async-start(), calls=%async_computation.2 | async-start | bytes 4325376 | tf_op jit(solution)/shard_map/all_gather | solution.py:65
  14.3 172.0 %all-gather.6.cloned.1.call-start = ((), (), s32[]{:S(2)}) async-start(), calls=%async_computation.3 | async-start | bytes 4325376 | tf_op jit(solution)/shard_map/all_gather | solution.py:68
  15.0 310.5 %all-gather.8.cloned.1.call-start = ((), (), s32[]{:S(2)}) async-start(), calls=%async_computation.4 | async-start | bytes 8650752 | tf_op jit(solution)/shard_map/all_gather | solution.py:103
  206.2 0.7 copy-start.4
  210.1 0.8 copy-start.1
  222.4 165.8 %reduce-scatter.5.cloned.1.call-start = ((), (), s32[]{:S(2)}) async-start(), calls=%async_computation.5 | async-start | bytes 4718592 | tf_op jit(solution)/shard_map/reduce_scatter | solution.py:119
  325.5 19.1 %copy-start.3 = (f32[2,1,512,128]{2,3,0,1:T(8,128)S(1)}, f32[2,1,512,128]{2,3,0,1:T(8,128)}, u32[]{:S(2)}) copy-start(f32[2,1,512,128]{2,3,0,1:T(8,128)} %convolution_bitcast_fusion.2) | copy-start | bytes 1572868
  352.3 269.8 %reduce-scatter.7.cloned.1.call-start = ((), (), s32[]{:S(2)}) async-start(), calls=%async_computation.6 | async-start | bytes 6488064
  365.4 1.1 copy-start.2
Sparse Core Ops, SparseCore 0:
  14.4 85.4 all-gather.3
  102.9 83.2 all-gather.5
  222.6 102.8 all-gather.7
  352.4 35.8 reduce-scatter.4
  392.7 229.3 reduce-scatter.6
where the time goes:
time: 630 us; the launch traced here: 629 us
  waiting for transfers between devices  505 us (80%)
  local copies, waits for them, and re-layouts  70.1 us (11%)
  matrix products  30.7 us (5%)
  between operations  14 us (2%)
  other arithmetic  8.57 us (1%)
    unnamed x6, waiting for transfers between devices  233 us
    all_gather x1, waiting for transfers between devices, per_device(): lax.all_gather(far_flat, 'ctx', axis=0, tiled=True)  94.2 us
    all_gather x1, waiting for transfers between devices, per_device(): lax.all_gather(value_flat, 'ctx', axis=0, tiled=True)  80 us
    all_gather x1, waiting for transfers between devices, per_device(): lax.all_gather(key_flat, 'ctx', axis=0, tiled=True)  77.1 us
    reshape x3, local copies, waits for them, and re-layouts, pick_rows(): shard_rows.reshape(row_count, head_count, width).transpose(1, 0, 2)  24.7 us
    reduce_scatter x1, waiting for transfers between devices, per_device(): lax.psum_scatter(lax.dot_general(w_qkv, grad_qkv, (((1,), (1,)), ((), ())...  20.7 us
    gather x4, local copies, waits for them, and re-layouts, pick_rows(): jnp.take_along_axis(by_head, jnp.clip(offset, 0, row_count - 1)[:, :, Non...  20.4 us
    unnamed x23, local copies, waits for them, and re-layouts  16.8 us
  transfers between devices with their start and end apart: 5, of which 5 were waited for; matrix products, arithmetic and copies ran while one was open for 6% of the time, Pallas kernels for 0%

commit v1 on v0

--- a/solution.py
+++ b/solution.py
@@ -62,7 +62,12 @@
     empty_rows = jnp.zeros((head_count, local_blocks, BLK, HD), jnp.bfloat16)
     first_row = jnp.int32(0)
     key_far = pick_rows(
-        empty_rows, lax.all_gather(key_flat, "ctx", axis=0, tiled=True), key_rows, first_row
+        empty_rows,
+        jnp.concatenate(
+            lax.all_to_all(jnp.stack([key_flat] * lax.axis_size("ctx")), "ctx", 0, 0), axis=0
+        ),
+        key_rows,
+        first_row,
     )
     value_far = pick_rows(
         empty_rows, lax.all_gather(value_flat, "ctx", axis=0, tiled=True), key_rows, first_row

time: 630 us -> 616 us (0.978)
  waiting for transfers between devices: 505 us -> 463 us
  local copies, waits for them, and re-layouts: 70.1 us -> 85.3 us
  starting transfers between devices: 0.38 us -> 11.9 us
    all_gather x1 -> x0, waiting for transfers between devices: 77.1 us -> none  [per_device(): lax.all_gather(key_flat, 'ctx', axis=0, tiled=True)]
    all_gather x1, waiting for transfers between devices: 80 us -> 118 us  [per_device(): lax.all_gather(value_flat, 'ctx', axis=0, tiled=True)]
    another operation x1 -> x4, local copies, waits for them, and re-layouts: 0.01 us -> 16.1 us  [the longest x2 13.7 us: pick_rows(): shard_rows.reshape(row_count, head_count, width).transpose(1, 0, 2)]
    all_to_all x0 -> x1, starting transfers between devices: none -> 11.6 us  [per_device(): lax.all_to_all(jnp.stack([key_flat] * lax.axis_size('ctx')), 'ctx', 0, 0)]
    all_to_all x0 -> x1, local copies, waits for them, and re-layouts: none -> 6.5 us  [per_device(): lax.all_to_all(jnp.stack([key_flat] * lax.axis_size('ctx')), 'ctx', 0, 0)]
    reshape x3 -> x2, local copies, waits for them, and re-layouts: 24.7 us -> 18.3 us  [pick_rows(): shard_rows.reshape(row_count, head_count, width).transpose(1, 0, 2)]
    unnamed x6 -> x5, waiting for transfers between devices: 233 us -> 232 us
  transfers between devices with their start and end apart: 5 -> 5, of which waited for: 5 -> 4; matrix products, arithmetic and copies ran while one was open for 6% -> 6% of each run, Pallas kernels for 0% -> 0%
where the time goes in v1:
time: 616 us; the launch traced here: 614 us
  waiting for transfers between devices  463 us (75%)
  local copies, waits for them, and re-layouts  85.3 us (14%)
  matrix products  30.8 us (5%)
  between operations  14 us (2%)
  starting transfers between devices  11.9 us (2%)
  other arithmetic  8.54 us (1%)
    unnamed x5, waiting for transfers between devices  232 us
    all_gather x1, waiting for transfers between devices, per_device(): lax.all_gather(value_flat, 'ctx', axis=0, tiled=True)  118 us
    all_gather x1, waiting for transfers between devices, per_device(): lax.all_gather(far_flat, 'ctx', axis=0, tiled=True)  92.7 us
    reduce_scatter x1, waiting for transfers between devices, per_device(): lax.psum_scatter(lax.dot_general(w_qkv, grad_qkv, (((1,), (1,)), ((), ())...  20.7 us
    gather x4, local copies, waits for them, and re-layouts, pick_rows(): jnp.take_along_axis(by_head, jnp.clip(offset, 0, row_count - 1)[:, :, Non...  20.4 us
    reshape x2, local copies, waits for them, and re-layouts, pick_rows(): shard_rows.reshape(row_count, head_count, width).transpose(1, 0, 2)  18.3 us
    unnamed x23, local copies, waits for them, and re-layouts  15.1 us
    another operation x2, local copies, waits for them, and re-layouts, pick_rows(): shard_rows.reshape(row_count, head_count, width).transpose(1, 0, 2)  13.7 us
  transfers between devices with their start and end apart: 5, of which 4 were waited for; matrix products, arithmetic and copies ran while one was open for 6% of the time, Pallas kernels for 0%

profile of v1, /device:TPU:8, one launch (start us, length us, event | category | flops | bytes accessed | tf_op | source)
XLA Modules:
  0.0 614.0 jit_solution(260116843082278978)
XLA Ops:
  7.2 0.0 all-gather.3.cloned.1.call-start
  7.2 1.5 copy-done
  8.8 4.6 convolution_convert_fusion.1
  13.3 0.2 copy.44
  13.5 0.7 fusion.41
  14.2 0.0 all-gather.3.cloned.1.call-update
  14.2 2.4 stack.15
  16.6 11.6 %all-to-all-start = ((bf16[32,256,256]{1,2,0:T(8,128)(2,1)}), bf16[32,256,256]{1,2,0:T(8,128)(2,1)}, u32[]{:S(2)}, u32[]{:S(2)}) async-start(bf16[32,256,256]{1,2,0:T(8,128)(2,1)} %stack.15), calls=%async_computation | async-start | bytes 8388608 | tf_op jit(solution)/shard_map/all_to_all | solution.py:67
  28.2 0.0 all-gather.5.cloned.1.call-start
  28.3 0.1 copy.75
  28.4 0.8 copy.74
  29.2 0.6 fusion.42
  29.8 0.6 or_bitcast_fusion
  30.4 0.1 shift_right_arithmetic.28
  30.5 0.1 copy.70
  30.6 0.8 copy.73
  31.4 0.9 shift_right_arithmetic.25
  32.3 1.3 copy.50
  33.6 0.6 and_bitcast_fusion
  34.2 0.6 compare_and_fusion.2
  34.9 117.9 %all-gather.3.cloned.1.call-done = bf16[8192,256]{0,1:T(8,128)(2,1)} async-done(((bf16[256,256]{0,1:T(8,128)(2,1)}), bf16[8192,256]{0,1:T(8,128)(2,1)}) %all-gather.3.cloned.1.call-update) | async-done | bytes 4194320 | tf_op jit(solution)/shard_map/all_gather | solution.py:73
  152.7 6.3 %copy.53 = bf16[8192,2,128]{2,0,1:T(8,128)(2,1)} copy(bf16[8192,2,128]{0,2,1:T(8,128)(2,1)} %bitcast.126) | data formatting | bytes 8388608 | tf_op jit(solution)/shard_map/reshape | solution.py:34
  159.0 6.5 %copy.48 = bf16[32,256,256]{1,0,2:T(8,128)(2,1)} copy(bf16[32,256,256]{1,2,0:T(8,128)(2,1)} %all-to-all-done) | data formatting | bytes 8388608 | tf_op jit(solution)/shard_map/all_to_all | solution.py:67
  165.5 7.4 %reshape_reshape.3 = bf16[8192,2,128]{0,2,1:T(8,128)(2,1)} reshape(bf16[32,256,256]{1,0,2:T(8,128)(2,1)} %copy.48) | data formatting | bytes 8388608 | tf_op jit(solution)/shard_map/reshape;reshape | solution.py:34
  173.0 6.3 %copy.49 = bf16[8192,2,128]{2,0,1:T(8,128)(2,1)} copy(bf16[8192,2,128]{0,2,1:T(8,128)(2,1)} %reshape_reshape.3) | data formatting | bytes 8388608 | tf_op jit(solution)/shard_map/reshape;reshape | solution.py:34
  179.3 6.7 %gather_fusion.2 = bf16[512,128]{1,0:T(8,128)(2,1)S(1)} fusion(bf16[2,8192,128]{2,1,0:T(8,128)(2,1)} %bitcast.124, s32[512]{0:T(512)S(1)} %bitcast.119), kind=kCustom, calls=%fused_computation.1.clone | custom fusion | bytes 266240 | tf_op jit(solution)/shard_map/jit(take_along_axis)/gather | solution.py:37
  185.9 6.8 %gather_fusion.1 = bf16[512,128]{1,0:T(8,128)(2,1)S(1)} fusion(bf16[2,8192,128]{2,1,0:T(8,128)(2,1)} %bitcast.125, s32[512]{0:T(512)S(1)} %bitcast.120), kind=kCustom, calls=%fused_computation.clone | custom fusion | bytes 266240 | tf_op jit(solution)/shard_map/jit(take_along_axis)/gather | solution.py:37
  192.7 0.2 fusion.25
  192.9 0.6 copy-done.5
  193.6 1.4 fusion.43
  194.9 0.3 exponential_reduce_fusion
  195.2 1.6 multiply_convert_fusion
  196.8 0.8 copy-done.1
  197.6 1.0 convolution_bitcast_fusion.2
  198.6 2.5 fusion.5
  201.2 5.3 convolution_bitcast_fusion.3
  206.5 1.0 slice.70
  207.5 1.0 slice.69
  208.4 0.7 pad_maximum_fusion
  209.2 0.0 all-gather.5.cloned.1.call-update
  209.2 0.2 reduce-scatter.5.cloned.1.call-start
  209.4 0.1 reshape.377
  209.5 0.1 reshape.379
  209.6 3.5 scatter_fusion
  213.1 0.2 multiply_reduce_fusion.1
  213.3 0.1 fusion.30
  213.4 0.1 compare_and_fusion.1
  213.5 4.7 fusion.7
  218.1 92.7 %all-gather.5.cloned.1.call-done = bf16[8192,512]{0,1:T(8,128)(2,1)} async-done(((bf16[256,512]{0,1:T(8,128)(2,1)}), bf16[8192,512]{0,1:T(8,128)(2,1)}) %all-gather.5.cloned.1.call-update) | async-done | bytes 8388624 | tf_op jit(solution)/shard_map/all_gather | solution.py:108
  310.9 12.0 %copy.60 = bf16[8192,2,256]{2,0,1:T(8,128)(2,1)} copy(bf16[8192,2,256]{0,2,1:T(8,128)(2,1)} %bitcast.123) | data formatting | bytes 16777216 | tf_op jit(solution)/shard_map/reshape | solution.py:34
  322.9 6.8 %gather_fusion = bf16[512,256]{1,0:T(8,128)(2,1)S(1)} fusion(bf16[2,8192,256]{2,1,0:T(8,128)(2,1)} %bitcast.122, s32[512]{0:T(512)S(1)} %bitcast.121), kind=kCustom, calls=%fused_computation.2 | custom fusion | bytes 528384 | tf_op jit(solution)/shard_map/jit(take_along_axis)/gather | solution.py:37
  329.7 0.1 copy.61
  329.9 1.0 fusion.21
  331.0 6.6 %convolution_bitcast_fusion = f32[4096,256]{0,1:T(8,128)} fusion(bf16[256,768]{0,1:T(8,128)(2,1)S(1)} %bitcast.128, bf16[4096,768]{1,0:T(8,128)(2,1)} %param.12), kind=kOutput, calls=%fused_computation.7 | convolution fusion | flops 1610612736 | bytes 10878976 | tf_op jit(solution)/shard_map/dot_general | solution.py:125
  337.6 0.0 reduce-scatter.5.cloned.1.call-update
  337.6 0.0 reduce-scatter.7.cloned.1.call-start
  337.7 4.5 fusion.1
  342.1 8.7 %copy.71 = bf16[4096,768]{1,0:T(8,128)(2,1)} copy(bf16[4096,768]{0,1:T(8,128)(2,1)} %fusion.1) | data formatting | bytes 12582912
  350.8 1.0 copy-done.2
  351.8 0.3 convolution_convert_fusion.3
  352.2 0.8 copy.63
  352.9 20.7 %reduce-scatter.5.cloned.1.call-done = f32[512,256]{0,1:T(8,128)} async-done(((f32[4096,256]{0,1:T(8,128)}), f32[512,256]{0,1:T(8,128)}) %reduce-scatter.5.cloned.1.call-update) | async-done | bytes 524304 | tf_op jit(solution)/shard_map/reduce_scatter | solution.py:124
  373.6 1.8 convert_bitcast_fusion
  375.4 232.1 %reduce-scatter.7.cloned.1.call-done = bf16[128,768]{1,0:T(8,128)(2,1)} async-done(((bf16[4096,768]{1,0:T(8,128)(2,1)}), bf16[128,768]{1,0:T(8,128)(2,1)}) %reduce-scatter.7.cloned.1.call-update) | async-done | bytes 196624
  (26 shorter events, 0.2 us)
Async XLA Ops:
  7.2 1.6 copy-start
  7.2 145.5 %all-gather.3.cloned.1.call-start = ((), (), s32[]{:S(2)}) async-start(), calls=%async_computation.3 | async-start | bytes 4325376 | tf_op jit(solution)/shard_map/all_gather | solution.py:73
  16.6 11.6 %copy-start.4 = (bf16[256,2,1,128]{0,3,2,1:T(8,128)(2,1)S(1)}, bf16[256,2,1,128]{0,3,2,1:T(8,128)(2,1)}, u32[]{:S(2)}) copy-start(bf16[256,2,1,128]{0,3,2,1:T(8,128)(2,1)} %get-tuple-element.13) | copy-start | bytes 393220
  16.6 12.5 %copy-start.7 = (s32[1,32]{1,0:T(1,128)S(1)}, s32[1,32]{1,0:T(1,128)}, u32[]{:S(2)}) copy-start(s32[1,32]{1,0:T(1,128)} %param.13) | copy-start | bytes 388
  16.6 13.9 %copy-start.6 = (bf16[256,256]{1,0:T(8,128)(2,1)S(1)}, bf16[256,256]{1,0:T(8,128)(2,1)}, u32[]{:S(2)}) copy-start(bf16[256,256]{1,0:T(8,128)(2,1)} %param.15) | copy-start | bytes 393220
  16.6 142.4 %all-to-all-start = ((bf16[32,256,256]{1,2,0:T(8,128)(2,1)}), bf16[32,256,256]{1,2,0:T(8,128)(2,1)}, u32[]{:S(2)}, u32[]{:S(2)}) async-start(bf16[32,256,256]{1,2,0:T(8,128)(2,1)} %stack.15), calls=%async_computation | async-start | bytes 8388608 | tf_op jit(solution)/shard_map/all_to_all | solution.py:67
  28.2 282.6 %all-gather.5.cloned.1.call-start = ((), (), s32[]{:S(2)}) async-start(), calls=%async_computation.4 | async-start | bytes 8650752 | tf_op jit(solution)/shard_map/all_gather | solution.py:108
  192.9 0.7 copy-start.5
  196.8 0.8 copy-start.1
  209.2 164.4 %reduce-scatter.5.cloned.1.call-start = ((), (), s32[]{:S(2)}) async-start(), calls=%async_computation.5 | async-start | bytes 4718592 | tf_op jit(solution)/shard_map/reduce_scatter | solution.py:124
  310.9 19.0 %copy-start.3 = (f32[2,1,512,128]{2,3,0,1:T(8,128)S(1)}, f32[2,1,512,128]{2,3,0,1:T(8,128)}, u32[]{:S(2)}) copy-start(f32[2,1,512,128]{2,3,0,1:T(8,128)} %convolution_bitcast_fusion.2) | copy-start | bytes 1572868
  337.6 269.8 %reduce-scatter.7.cloned.1.call-start = ((), (), s32[]{:S(2)}) async-start(), calls=%async_computation.6 | async-start | bytes 6488064
  350.8 1.1 copy-start.2
Sparse Core Ops, SparseCore 0:
  14.3 138.3 all-gather.2
  209.3 101.5 all-gather.4
  337.7 35.8 reduce-scatter.4
  378.0 229.3 reduce-scatter.6
